TPU v7x, 256 devices: a whole 4x4x8 slice. The times are simulated.
256 devices in a mesh: dp: 16 (over y_lo, x, core), tensor: 16 (over z, y_hi).
Axes of the slice: x: 4, y: 4 (y_hi: 2, y_lo: 2; y = y_hi * 2 + y_lo), z: 8, core: 2. Of those that a mesh axis runs over, the one named last changes fastest.
Arguments:
- gate_pre: bfloat16 [8192, 14336], P('dp', 'tensor'), may hold values from -6 to 6
- up_pre: bfloat16 [8192, 14336], P('dp', 'tensor'), may hold values from -6 to 6
- grad_out: bfloat16 [8192, 4096], P(('dp', 'tensor')), may hold values from -24 to 24
- codes: bfloat16 [14336, 4096], P('tensor'), as said below
- scales: int32 [448, 4096], P('tensor'), may hold values from 117 to 120
Outputs:
- out: bfloat16 [8192, 4096], P(('dp', 'tensor'))
- grad_gate: bfloat16 [8192, 14336], P('dp', 'tensor')
- grad_up: bfloat16 [8192, 14336], P('dp', 'tensor')
- grad_weight: bfloat16 [14336, 4096], P('tensor', 'dp')
Inputs may be any that keep to these rules, and one draw needn't show every extreme that they name: `codes`: every entry is an FP8 E4M3 normal value (sign, exponent field 4 to 9, three mantissa bits), held exactly.
All inputs are finite; a program needn't handle non-finite values.
Results may differ from a plain program's by a relative error of at most 0.022.
Values may be sent and summed in bfloat16 or wider, within the bound.
No kernel may reach another device: no remote copies, remote signals or barrier semaphores. Data moves between devices by JAX's collectives and lax.ppermute only.
A program may use at most 128 MiB of HBM per device.

v0:
```python
import jax
import jax.numpy as jnp
from jax import lax
from jax.experimental.layout import Layout, with_layout_constraint
from jax.sharding import Mesh, PartitionSpec as P

DP = ("dy", "dx", "dc")
TP = ("tz", "ty")


def decode(codes, scales):
    factor = jnp.exp2(scales.astype(jnp.float32) - 127.0).astype(jnp.bfloat16)
    blocks = codes.reshape(scales.shape[0], 32, codes.shape[1]) * factor[:, None, :]
    return blocks.reshape(codes.shape)


def exchange(value, axis, size, shift):
    perm = [(i, (i + shift) % size) for i in range(size)]
    return lax.ppermute(value, axis, perm)


def weight_gradient(hidden, cotangent):
    n_x = cotangent.shape[1] // 1024
    width = 256
    partial = lax.dot_general(
        cotangent, hidden, (((0,), (0,)), ((), ())), preferred_element_type=jnp.float32
    ).astype(jnp.bfloat16)
    partial = with_layout_constraint(partial, Layout(major_to_minor=(0, 1)))
    parts = partial.reshape(2, n_x, 2, width, partial.shape[1])
    dc = lax.axis_index("dc")
    mine = jnp.take(parts, dc, axis=2)
    arrived = exchange(jnp.take(parts, 1 - dc, axis=2), "dc", 2, 1)
    total = mine.astype(jnp.float32) + arrived.astype(jnp.float32)
    total = with_layout_constraint(total, Layout(major_to_minor=(0, 1, 2, 3)))
    sent = total.astype(jnp.bfloat16)
    dx = lax.axis_index("dx")
    acc = jnp.take(total, dx, axis=1)
    for shift in range(1, n_x):
        block = jnp.take(sent, (dx + shift) % n_x, axis=1)
        acc = acc + exchange(block, "dx", n_x, shift).astype(jnp.float32)
    dy = lax.axis_index("dy")
    sent = acc.astype(jnp.bfloat16)
    acc = jnp.take(acc, dy, axis=0) + exchange(jnp.take(sent, 1 - dy, axis=0), "dy", 2, 1).astype(
        jnp.float32
    )
    acc = with_layout_constraint(acc.astype(jnp.bfloat16), Layout(major_to_minor=(0, 1)))
    return acc.T


def per_device(gate_pre, up_pre, grad_out, codes, scales):
    weight = decode(codes, scales)
    gate_value = gate_pre.astype(jnp.float32)
    up_value = up_pre.astype(jnp.float32)
    sigmoid_gate = jax.nn.sigmoid(gate_value)
    hidden = (gate_value * sigmoid_gate * up_value).astype(jnp.bfloat16)
    partial_out = jnp.dot(hidden, weight, preferred_element_type=jnp.float32).astype(jnp.bfloat16)
    out = lax.psum_scatter(partial_out, "tz", scatter_dimension=0, tiled=True)
    rows = out.shape[0] // 2
    ty = lax.axis_index("ty")
    out = lax.dynamic_slice_in_dim(out, ty * rows, rows, 0).astype(jnp.float32) + exchange(
        lax.dynamic_slice_in_dim(out, (1 - ty) * rows, rows, 0), "ty", 2, 1
    ).astype(jnp.float32)
    out = out.astype(jnp.bfloat16)
    cotangent = lax.all_gather(grad_out, "ty", axis=0, tiled=True)
    cotangent = lax.all_gather(cotangent, "tz", axis=0, tiled=True)
    grad_hidden = lax.dot_general(
        cotangent, weight, (((1,), (1,)), ((), ())), preferred_element_type=jnp.float32
    )
    grad_weight = weight_gradient(hidden, cotangent)
    grad_gate = (
        grad_hidden * up_value * sigmoid_gate * (1.0 + gate_value * (1.0 - sigmoid_gate))
    ).astype(jnp.bfloat16)
    grad_up = (grad_hidden * gate_value * sigmoid_gate).astype(jnp.bfloat16)
    return (out, grad_gate, grad_up, grad_weight)


def split_mesh(mesh):
    n_dp, n_tensor = (mesh.shape["dp"], mesh.shape["tensor"])
    devices = mesh.devices.reshape(2, n_dp // 4, 2, n_tensor // 2, 2)
    return Mesh(devices, DP + TP)


def solution(mesh):
    fine = split_mesh(mesh)
    in_specs = (P(DP, TP), P(DP, TP), P(DP + TP, None), P(TP, None), P(TP, None))
    out_specs = (P(DP + TP, None), P(DP, TP), P(DP, TP), P(TP, DP))
    return jax.shard_map(
        per_device, mesh=fine, in_specs=in_specs, out_specs=out_specs, check_vma=False
    )
```

profile of v0, /device:TPU:1, one launch (start us, length us, event | category | flops | bytes accessed | tf_op | source)
XLA Modules:
  0.0 170.8 jit_solution(15946947193299180030)
XLA Ops:
  7.2 12.1 %all_gather.6 = bf16[64,4096]{1,0:T(8,128)(2,1)} all-gather(bf16[32,4096]{1,0:T(8,128)(2,1)} %param.11), channel_id=1, replica_groups=mesh['dy'=2,'dx'=4,'dc'=2,'tz'=8,'ty'=2] {'ty'}, dimensions={0}, use_global_device_ids=true | all-gather | bytes 786432 | tf_op jit(solution)/shard_map/all_gather | solution.py:64
  19.5 1.3 copy.17
  20.8 1.3 copy.16
  22.0 0.1 exponential_convert_fusion
  22.2 3.7 %bitcast_multiply_fusion = bf16[896,4096]{1,0:T(8,128)(2,1)S(1)} fusion(bf16[896,4096]{1,0:T(8,128)(2,1)} %param.12, bf16[28,4096]{1,0:T(8,128)(2,1)S(1)} %exponential_convert_fusion), kind=kLoop, calls=%fused_computation | loop fusion | flops 3670016 | bytes 14909440 | tf_op jit(solution)/shard_map/mul | solution.py:13
  25.8 2.9 %copy-done.1 = bf16[896,4096]{1,0:T(8,128)(2,1)} copy-done((bf16[896,4096]{1,0:T(8,128)(2,1)}, bf16[896,4096]{1,0:T(8,128)(2,1)S(1)}, u32[]{:S(2)}) %copy-start.1) | copy-done | bytes 7340056
  28.8 8.1 %convolution_convert_fusion.1 = bf16[512,4096]{1,0:T(8,128)(2,1)} fusion(bf16[896,4096]{1,0:T(8,128)(2,1)S(1)} %bitcast_multiply_fusion, bf16[512,896]{0,1:T(8,128)(2,1)} %copy.17, bf16[512,896]{0,1:T(8,128)(2,1)} %copy.16), kind=kOutput, calls=%fused_computation.3 | convolution fusion | flops 3763863552 | bytes 13369344 | tf_op jit(solution)/shard_map/dot_general | solution.py:56
  36.9 39.5 %all-gather.2.cloned.1.call-done = bf16[512,4096]{1,0:T(8,128)(2,1)} async-done(((bf16[64,4096]{1,0:T(8,128)(2,1)}), bf16[512,4096]{1,0:T(8,128)(2,1)}) %all-gather.2.cloned.1.call-update) | async-done | bytes 4194320 | tf_op jit(solution)/shard_map/all_gather | solution.py:65
  76.5 7.2 %convolution_convert_fusion = bf16[896,4096]{0,1:T(8,128)(2,1)S(1)} fusion(bf16[512,4096]{1,0:T(8,128)(2,1)} %all-gather.2.cloned.1.call-done, bf16[512,896]{0,1:T(8,128)(2,1)S(1)} %copy-done.5, bf16[512,896]{0,1:T(8,128)(2,1)S(1)} %copy-done.7), kind=kOutput, calls=%fused_computation.2 | convolution fusion | flops 3765436416 | bytes 13369344 | tf_op jit(solution)/shard_map/dot_general | solution.py:25
  83.7 3.0 %copy-done.2 = bf16[896,4096]{0,1:T(8,128)(2,1)} copy-done((bf16[896,4096]{0,1:T(8,128)(2,1)}, bf16[896,4096]{0,1:T(8,128)(2,1)S(1)}, u32[]{:S(2)}) %copy-start.2) | copy-done | bytes 7340056
  86.7 2.3 %fusion = bf16[2,4,256,896]{3,2,1,0:T(8,128)(2,1)} fusion(bf16[2,4,2,256,896]{4,3,2,1,0:T(8,128)(2,1)S(1)} %bitcast.52, s32[]{:T(128)S(6)} %select_n.90, pred[]{:T(512)S(6)} %and.53), kind=kLoop, calls=%fused_computation.5 | loop fusion | flops 1835008 | bytes 7340037 | tf_op jit(solution)/shard_map/jit(_take)/select_n | solution.py:32
  89.0 0.8 collective-permute-start.1
  89.8 6.4 %collective-permute-done.1 = bf16[2,4,256,896]{3,2,1,0:T(8,128)(2,1)} collective-permute-done((bf16[2,4,256,896]{3,2,1,0:T(8,128)(2,1)}, bf16[2,4,256,896]{3,2,1,0:T(8,128)(2,1)}, u32[]{:S(2)}, u32[]{:S(2)}) %collective-permute-start.1) | collective-permute-done | bytes 3670048 | tf_op jit(solution)/shard_map/ppermute | solution.py:19
  96.2 4.4 %convert_add_fusion = f32[2,4,256,896]{3,2,1,0:T(8,128)S(1)} fusion(bf16[2,4,256,896]{3,2,1,0:T(8,128)(2,1)} %collective-permute-done.1, bf16[2,4,2,256,896]{4,3,2,1,0:T(8,128)(2,1)} %bitcast.53, s32[]{:T(128)S(6)} %select_n.88, pred[]{:T(512)S(6)} %and.52), kind=kLoop, calls=%fused_computation.1 | loop fusion | flops 7340032 | bytes 14680069 | tf_op jit(solution)/shard_map/add | solution.py:33
  100.6 1.6 select_bitcast_fusion.2
  102.2 2.4 %collective-permute-start.4 = (bf16[2,256,896]{2,1,0:T(8,128)(2,1)}, bf16[2,256,896]{2,1,0:T(8,128)(2,1)}, u32[]{:S(2)}, u32[]{:S(2)}) collective-permute-start(bf16[2,256,896]{2,1,0:T(8,128)(2,1)} %get-tuple-element.70), channel_id=1, source_target_pairs={{0,96},{32,0},{64,32},{96,64},{1,97},{33,1},{65,33},{97,65},{2,98}... | collective-permute-start | bytes 2752520 | tf_op jit(solution)/shard_map/ppermute | solution.py:19
  104.6 0.6 collective-permute-start.3
  105.2 0.6 collective-permute-start.2
  105.8 5.9 %fusion.11 = (bf16[512,896]{0,1:T(8,128)(2,1)}, bf16[512,896]{0,1:T(8,128)(2,1)}) fusion(bf16[512,896]{0,1:T(8,128)(2,1)S(1)} %copy-done.8, bf16[512,896]{0,1:T(8,128)(2,1)S(1)} %copy-done.6, bf16[896,4096]{1,0:T(8,128)(2,1)S(1)} %bitcast.51, bf16[512,4096]{1,0:T(8,128)(2,1)S(1)} %copy-done.12), kind=kOutput, calls=%fused_computation.23 | convolution fusion | flops 3764977664 | bytes 15204352 | tf_op jit(solution)/shard_map/dot_general | solution.py:66
  111.6 2.3 %copy.22 = bf16[512,896]{1,0:T(8,128)(2,1)} copy(bf16[512,896]{0,1:T(8,128)(2,1)} %get-tuple-element.73) | data formatting | bytes 1835008
  114.0 1.3 copy.23
  115.2 17.8 %reduce-scatter.2.cloned.1.call-done = bf16[64,4096]{1,0:T(8,128)(2,1)} async-done(((bf16[512,4096]{1,0:T(8,128)(2,1)}), bf16[64,4096]{1,0:T(8,128)(2,1)}) %reduce-scatter.2.cloned.1.call-update) | async-done | bytes 524304 | tf_op jit(solution)/shard_map/reduce_scatter | solution.py:57
  133.0 1.0 constant_dynamic-slice_fusion
  134.0 2.8 %collective-permute-start = (bf16[32,4096]{1,0:T(8,128)(2,1)S(1)}, bf16[32,4096]{1,0:T(8,128)(2,1)S(1)}, u32[]{:S(2)}, u32[]{:S(2)}) collective-permute-start(bf16[32,4096]{1,0:T(8,128)(2,1)S(1)} %constant_dynamic-slice_fusion), channel_id=1, source_target_pairs={{0,1},{1,0},{2,3},{3,2},{4,5},{5,4},{6,7},{7,6},{8,9},{9,8},{10,11... | collective-permute-start | bytes 786440 | tf_op jit(solution)/shard_map/ppermute | solution.py:19
  136.9 11.5 %collective-permute-done.2 = bf16[2,256,896]{2,1,0:T(8,128)(2,1)} collective-permute-done((bf16[2,256,896]{2,1,0:T(8,128)(2,1)}, bf16[2,256,896]{2,1,0:T(8,128)(2,1)}, u32[]{:S(2)}, u32[]{:S(2)}) %collective-permute-start.2) | collective-permute-done | bytes 917536 | tf_op jit(solution)/shard_map/ppermute | solution.py:19
  148.4 2.8 %fusion.13 = f32[2,256,896]{2,1,0:T(8,128)S(1)} fusion(s32[]{:T(128)S(6)} %select_n.60, bf16[2,256,896]{2,1,0:T(8,128)(2,1)} %collective-permute-done.4, bf16[2,256,896]{2,1,0:T(8,128)(2,1)} %collective-permute-done.3, bf16[2,256,896]{2,1,0:T(8,128)(2,1)} %collective-permute-done.2, pred[]{:T(512)S(6)} %and.50, f32[2,4,256,896]{3,2,1,0:T(8,128)} %copy-done), kind=kLoop, calls=%fused_computation.26 | loop fusion | flops 3211264 | bytes 6422533 | tf_op jit(solution)/shard_map/add | solution.py:40
  151.1 0.1 fusion.17
  151.2 1.3 collective-permute-start.5
  152.5 0.8 add_convert_fusion
  153.3 9.6 %collective-permute-done.5 = bf16[256,896]{1,0:T(8,128)(2,1)S(1)} collective-permute-done((bf16[256,896]{1,0:T(8,128)(2,1)S(1)}, bf16[256,896]{1,0:T(8,128)(2,1)S(1)}, u32[]{:S(2)}, u32[]{:S(2)}) %collective-permute-start.5) | collective-permute-done | bytes 458784 | tf_op jit(solution)/shard_map/ppermute | solution.py:19
  162.9 0.1 fusion.15
  163.0 1.0 copy.24
  (36 shorter events, 0.2 us)
Async XLA Ops:
  7.2 12.3 %copy-start.3 = (bf16[512,896]{1,0:T(8,128)(2,1)S(1)}, bf16[512,896]{1,0:T(8,128)(2,1)}, u32[]{:S(2)}) copy-start(bf16[512,896]{1,0:T(8,128)(2,1)} %param.10) | copy-start | bytes 2752516
  7.2 13.6 %copy-start.4 = (bf16[512,896]{1,0:T(8,128)(2,1)S(1)}, bf16[512,896]{1,0:T(8,128)(2,1)}, u32[]{:S(2)}) copy-start(bf16[512,896]{1,0:T(8,128)(2,1)} %param.9) | copy-start | bytes 2752516
  7.2 69.3 %all-gather.2.cloned.1.call-start = ((), (), s32[]{:S(2)}) async-start(), calls=%async_computation.2 | async-start | bytes 4718592 | tf_op jit(solution)/shard_map/all_gather | solution.py:65
  19.4 2.6 %copy-start.10 = (s32[28,4096]{1,0:T(8,128)S(1)}, s32[28,4096]{1,0:T(8,128)}, u32[]{:S(2)}) copy-start(s32[28,4096]{1,0:T(8,128)} %param.13) | copy-start | bytes 1376260
  19.4 113.6 %reduce-scatter.2.cloned.1.call-start = ((), (), s32[]{:S(2)}) async-start(), calls=%async_computation.1 | async-start | bytes 4718592 | tf_op jit(solution)/shard_map/reduce_scatter | solution.py:57
  25.8 2.9 %copy-start.1 = (bf16[896,4096]{1,0:T(8,128)(2,1)}, bf16[896,4096]{1,0:T(8,128)(2,1)S(1)}, u32[]{:S(2)}) copy-start(bf16[896,4096]{1,0:T(8,128)(2,1)S(1)} %bitcast_multiply_fusion) | copy-start | bytes 22020100
  36.9 39.6 %copy-start.5 = (bf16[512,896]{0,1:T(8,128)(2,1)S(1)}, bf16[512,896]{0,1:T(8,128)(2,1)}, u32[]{:S(2)}) copy-start(bf16[512,896]{0,1:T(8,128)(2,1)} %copy.17) | copy-start | bytes 2752516
  36.9 39.6 %copy-start.7 = (bf16[512,896]{0,1:T(8,128)(2,1)S(1)}, bf16[512,896]{0,1:T(8,128)(2,1)}, u32[]{:S(2)}) copy-start(bf16[512,896]{0,1:T(8,128)(2,1)} %copy.16) | copy-start | bytes 2752516
  83.7 3.0 %copy-start.2 = (bf16[896,4096]{0,1:T(8,128)(2,1)}, bf16[896,4096]{0,1:T(8,128)(2,1)S(1)}, u32[]{:S(2)}) copy-start(bf16[896,4096]{0,1:T(8,128)(2,1)S(1)} %convolution_convert_fusion) | copy-start | bytes 22020100
  86.7 19.1 %slice-start = ((s8[7340032]{0:T(1024)(128)(4,1)}), s8[3145728]{0:T(1024)(128)(4,1)S(1)}, s32[]{:S(2)}) async-start(s8[7340032]{0:T(1024)(128)(4,1)} %bitcast.50), calls=%async_computation.3 | async-start | bytes 6291456
  89.0 7.2 %collective-permute-start.1 = (bf16[2,4,256,896]{3,2,1,0:T(8,128)(2,1)}, bf16[2,4,256,896]{3,2,1,0:T(8,128)(2,1)}, u32[]{:S(2)}, u32[]{:S(2)}) collective-permute-start(bf16[2,4,256,896]{3,2,1,0:T(8,128)(2,1)} %fusion), channel_id=1, source_target_pairs={{0,16},{16,0},{1,17},{17,1},{2,18},{18,2},{3,19},{19,3},{4,20},{20... | collective-permute-start | bytes 11010056 | tf_op jit(solution)/shard_map/ppermute | solution.py:19
  89.8 15.9 %slice-start.1 = ((s8[7340032]{0:T(1024)(128)(4,1)}), s8[4194304]{0:T(1024)(128)(4,1)S(1)}, s32[]{:S(2)}) async-start(s8[7340032]{0:T(1024)(128)(4,1)} %bitcast.50), calls=%async_computation.4 | async-start | bytes 8388608
  96.2 9.6 %copy-start.12 = (bf16[512,4096]{1,0:T(8,128)(2,1)S(1)}, bf16[512,4096]{1,0:T(8,128)(2,1)}, u32[]{:S(2)}) copy-start(bf16[512,4096]{1,0:T(8,128)(2,1)} %all-gather.2.cloned.1.call-done) | copy-start | bytes 12582916
  100.6 11.1 %copy-start = (f32[2,4,256,896]{3,2,1,0:T(8,128)}, f32[2,4,256,896]{3,2,1,0:T(8,128)S(1)}, u32[]{:S(2)}) copy-start(f32[2,4,256,896]{3,2,1,0:T(8,128)S(1)} %convert_add_fusion) | copy-start | bytes 22020100
  100.6 5.2 %copy-start.6 = (bf16[512,896]{0,1:T(8,128)(2,1)S(1)}, bf16[512,896]{0,1:T(8,128)(2,1)}, u32[]{:S(2)}) copy-start(bf16[512,896]{0,1:T(8,128)(2,1)} %copy.17) | copy-start | bytes 2752516
  100.6 5.2 %copy-start.8 = (bf16[512,896]{0,1:T(8,128)(2,1)S(1)}, bf16[512,896]{0,1:T(8,128)(2,1)}, u32[]{:S(2)}) copy-start(bf16[512,896]{0,1:T(8,128)(2,1)} %copy.16) | copy-start | bytes 2752516
  102.2 34.6 %collective-permute-start.4 = (bf16[2,256,896]{2,1,0:T(8,128)(2,1)}, bf16[2,256,896]{2,1,0:T(8,128)(2,1)}, u32[]{:S(2)}, u32[]{:S(2)}) collective-permute-start(bf16[2,256,896]{2,1,0:T(8,128)(2,1)} %get-tuple-element.70), channel_id=1, source_target_pairs={{0,96},{32,0},{64,32},{96,64},{1,97},{33,1},{65,33},{97,65},{2,98}... | collective-permute-start | bytes 2752520 | tf_op jit(solution)/shard_map/ppermute | solution.py:19
  104.6 32.2 %collective-permute-start.3 = (bf16[2,256,896]{2,1,0:T(8,128)(2,1)}, bf16[2,256,896]{2,1,0:T(8,128)(2,1)}, u32[]{:S(2)}, u32[]{:S(2)}) collective-permute-start(bf16[2,256,896]{2,1,0:T(8,128)(2,1)} %get-tuple-element.71), channel_id=1, source_target_pairs={{0,64},{32,96},{64,0},{96,32},{1,65},{33,97},{65,1},{97,33},{2,66}... | collective-permute-start | bytes 2752520 | tf_op jit(solution)/shard_map/ppermute | solution.py:19
  105.2 43.2 %collective-permute-start.2 = (bf16[2,256,896]{2,1,0:T(8,128)(2,1)}, bf16[2,256,896]{2,1,0:T(8,128)(2,1)}, u32[]{:S(2)}, u32[]{:S(2)}) collective-permute-start(bf16[2,256,896]{2,1,0:T(8,128)(2,1)} %get-tuple-element.69), channel_id=1, source_target_pairs={{0,32},{32,64},{64,96},{96,0},{1,33},{33,65},{65,97},{97,1},{2,34}... | collective-permute-start | bytes 2752520 | tf_op jit(solution)/shard_map/ppermute | solution.py:19
  111.6 2.3 %copy-start.9 = (bf16[512,896]{0,1:T(8,128)(2,1)S(1)}, bf16[512,896]{0,1:T(8,128)(2,1)}, u32[]{:S(2)}) copy-start(bf16[512,896]{0,1:T(8,128)(2,1)} %get-tuple-element.72) | copy-start | bytes 2752516
  134.0 18.5 %copy-start.11 = (bf16[64,4096]{1,0:T(8,128)(2,1)S(1)}, bf16[64,4096]{1,0:T(8,128)(2,1)}, u32[]{:S(2)}) copy-start(bf16[64,4096]{1,0:T(8,128)(2,1)} %reduce-scatter.2.cloned.1.call-done) | copy-start | bytes 1572868
  134.0 18.5 %collective-permute-start = (bf16[32,4096]{1,0:T(8,128)(2,1)S(1)}, bf16[32,4096]{1,0:T(8,128)(2,1)S(1)}, u32[]{:S(2)}, u32[]{:S(2)}) collective-permute-start(bf16[32,4096]{1,0:T(8,128)(2,1)S(1)} %constant_dynamic-slice_fusion), channel_id=1, source_target_pairs={{0,1},{1,0},{2,3},{3,2},{4,5},{5,4},{6,7},{7,6},{8,9},{9,8},{10,11... | collective-permute-start | bytes 786440 | tf_op jit(solution)/shard_map/ppermute | solution.py:19
  151.2 11.7 %collective-permute-start.5 = (bf16[256,896]{1,0:T(8,128)(2,1)S(1)}, bf16[256,896]{1,0:T(8,128)(2,1)S(1)}, u32[]{:S(2)}, u32[]{:S(2)}) collective-permute-start(bf16[256,896]{1,0:T(8,128)(2,1)S(1)} %fusion.17), channel_id=1, source_target_pairs={{0,128},{128,0},{1,129},{129,1},{2,130},{130,2},{3,131},{131,3},{4... | collective-permute-start | bytes 1376264 | tf_op jit(solution)/shard_map/ppermute | solution.py:19
Sparse Core Ops, SparseCore 0:
  19.5 56.8 all-gather.1
  79.0 54.0 reduce-scatter.1
where the time goes:
time: 171 us
  waiting for transfers between devices  84.9 us (50%)
  matrix products  21.2 us (12%)
  other arithmetic  15.8 us (9%)
  between operations  14.2 us (8%)
  local copies, waits for them, and re-layouts  14.1 us (8%)
  blocking collectives  12.1 us (7%)
  starting transfers between devices  8.59 us (5%)
    all_gather x1, waiting for transfers between devices, per_device(): cotangent = lax.all_gather(cotangent, 'tz', axis=0, tiled=True)  39.5 us
    ppermute x6, waiting for transfers between devices, exchange(): return lax.ppermute(value, axis, perm)  27.5 us
    reduce_scatter x1, waiting for transfers between devices, per_device(): out = lax.psum_scatter(partial_out, 'tz', scatter_dimension=0, tiled=True)  17.8 us
    unnamed x35, local copies, waits for them, and re-layouts  13.1 us
    all_gather x1, blocking collectives, per_device(): cotangent = lax.all_gather(grad_out, 'ty', axis=0, tiled=True)  12.1 us
    ppermute x6, starting transfers between devices, exchange(): return lax.ppermute(value, axis, perm)  8.51 us
    dot_general x1, matrix products, per_device(): jnp.dot(hidden, weight, preferred_element_type=jnp.float32)  8.1 us
    dot_general x1, matrix products, weight_gradient(): lax.dot_general(cotangent, hidden, (((0,), (0,)), ((), ())), preferred_el...  7.19 us
  transfers between devices with their start and end apart: 8, of which 5 were waited for; matrix products, arithmetic and copies ran while one was open for 26% of the time, Pallas kernels for 0%

commit v1 on v0

--- a/solution.py
+++ b/solution.py
@@ -61,7 +61,9 @@
         lax.dynamic_slice_in_dim(out, (1 - ty) * rows, rows, 0), "ty", 2, 1
     ).astype(jnp.float32)
     out = out.astype(jnp.bfloat16)
-    cotangent = lax.all_gather(grad_out, "ty", axis=0, tiled=True)
+    answer = jnp.stack([grad_out for _ in range(lax.psum(1, axis_name="ty"))], 0)
+    front = lax.all_to_all(answer, axis_name="ty", split_axis=0, concat_axis=0)
+    cotangent = jnp.concatenate(front, 0)
     cotangent = lax.all_gather(cotangent, "tz", axis=0, tiled=True)
     grad_hidden = lax.dot_general(
         cotangent, weight, (((1,), (1,)), ((), ())), preferred_element_type=jnp.float32

time: 171 us -> 176 us (1.029)
  waiting for transfers between devices: 84.9 us -> 90.7 us
  local copies, waits for them, and re-layouts: 14.1 us -> 10.9 us
    all_to_all x0 -> x1, blocking collectives: none -> 13.1 us  [per_device(): front = lax.all_to_all(answer, axis_name='ty', split_axis=0, concat_axis=0)]
    all_gather x1 -> x0, blocking collectives: 12.1 us -> none  [per_device(): cotangent = lax.all_gather(grad_out, 'ty', axis=0, tiled=True)]
    unnamed x35 -> x25, local copies, waits for them, and re-layouts: 13.1 us -> 9.98 us
    ppermute x6, waiting for transfers between devices: 27.5 us -> 30.5 us  [exchange(): return lax.ppermute(value, axis, perm)]
    all_gather x1, waiting for transfers between devices: 39.5 us -> 42.2 us  [per_device(): cotangent = lax.all_gather(cotangent, 'tz', axis=0, tiled=True)]
  transfers between devices with their start and end apart: 8 -> 8, of which waited for: 5 -> 5; matrix products, arithmetic and copies ran while one was open for 26% -> 22% of each run, Pallas kernels for 0% -> 0%
where the time goes in v1:
time: 176 us
  waiting for transfers between devices  90.7 us (52%)
  matrix products  21.3 us (12%)
  other arithmetic  16.9 us (10%)
  between operations  14.2 us (8%)
  blocking collectives  13.1 us (7%)
  local copies, waits for them, and re-layouts  10.9 us (6%)
  starting transfers between devices  8.59 us (5%)
    all_gather x1, waiting for transfers between devices, per_device(): cotangent = lax.all_gather(cotangent, 'tz', axis=0, tiled=True)  42.2 us
    ppermute x6, waiting for transfers between devices, exchange(): return lax.ppermute(value, axis, perm)  30.5 us
    reduce_scatter x1, waiting for transfers between devices, per_device(): out = lax.psum_scatter(partial_out, 'tz', scatter_dimension=0, tiled=True)  18 us
    all_to_all x1, blocking collectives, per_device(): front = lax.all_to_all(answer, axis_name='ty', split_axis=0, concat_axis=0)  13.1 us
    unnamed x25, local copies, waits for them, and re-layouts  9.98 us
    ppermute x6, starting transfers between devices, exchange(): return lax.ppermute(value, axis, perm)  8.51 us
    dot_general x1, matrix products, per_device(): jnp.dot(hidden, weight, preferred_element_type=jnp.float32)  7.76 us
    dot_general x1, matrix products, weight_gradient(): lax.dot_general(cotangent, hidden, (((0,), (0,)), ((), ())), preferred_el...  7.21 us
  transfers between devices with their start and end apart: 8, of which 5 were waited for; matrix products, arithmetic and copies ran while one was open for 22% of the time, Pallas kernels for 0%

profile of v1, /device:TPU:1, one launch (start us, length us, event | category | flops | bytes accessed | tf_op | source)
XLA Modules:
  0.0 175.6 jit_solution(11734605136930083433)
XLA Ops:
  7.2 0.0 all-gather.2.cloned.1.call-start
  7.2 1.1 pad_maximum_fusion
  8.4 13.1 %all_to_all.5 = bf16[2,32,4096]{2,1,0:T(8,128)(2,1)} all-to-all(bf16[2,32,4096]{2,1,0:T(8,128)(2,1)S(1)} %pad_maximum_fusion), channel_id=1, replica_groups=mesh['dy'=2,'dx'=4,'dc'=2,'tz'=8,'ty'=2] {'ty'}, dimensions={0} | all-to-all | bytes 1048576 | tf_op jit(solution)/shard_map/all_to_all | solution.py:65
  21.4 0.0 reduce-scatter.2.cloned.1.call-start
  21.5 0.1 exponential_convert_fusion
  21.6 3.7 %bitcast_multiply_fusion = bf16[896,4096]{1,0:T(8,128)(2,1)S(1)} fusion(bf16[896,4096]{1,0:T(8,128)(2,1)} %param.12, bf16[28,4096]{1,0:T(8,128)(2,1)S(1)} %exponential_convert_fusion), kind=kLoop, calls=%fused_computation | loop fusion | flops 3670016 | bytes 14909440 | tf_op jit(solution)/shard_map/mul | solution.py:13
  25.3 2.9 %copy-done.1 = bf16[896,4096]{1,0:T(8,128)(2,1)} copy-done((bf16[896,4096]{1,0:T(8,128)(2,1)}, bf16[896,4096]{1,0:T(8,128)(2,1)S(1)}, u32[]{:S(2)}) %copy-start.1) | copy-done | bytes 7340056
  28.2 7.8 %convolution_convert_fusion.1 = bf16[512,4096]{1,0:T(8,128)(2,1)} fusion(bf16[896,4096]{1,0:T(8,128)(2,1)S(1)} %bitcast_multiply_fusion, bf16[512,896]{1,0:T(8,128)(2,1)} %param.10, bf16[512,896]{1,0:T(8,128)(2,1)} %param.9), kind=kOutput, calls=%fused_computation.3 | convolution fusion | flops 3763863552 | bytes 13369344 | tf_op jit(solution)/shard_map/dot_general | solution.py:56
  36.0 42.2 %all-gather.2.cloned.1.call-done = bf16[512,4096]{1,0:T(8,128)(2,1)} async-done(((bf16[64,4096]{1,0:T(8,128)(2,1)}), bf16[512,4096]{1,0:T(8,128)(2,1)}) %all-gather.2.cloned.1.call-update) | async-done | bytes 4194320 | tf_op jit(solution)/shard_map/all_gather | solution.py:67
  78.2 7.2 %convolution_convert_fusion = bf16[4096,896]{1,0:T(8,128)(2,1)S(1)} fusion(bf16[512,4096]{1,0:T(8,128)(2,1)} %all-gather.2.cloned.1.call-done, bf16[512,896]{1,0:T(8,128)(2,1)S(1)} %copy-done.6, bf16[512,896]{1,0:T(8,128)(2,1)S(1)} %copy-done.8), kind=kOutput, calls=%fused_computation.2 | convolution fusion | flops 3765436416 | bytes 13369344 | tf_op jit(solution)/shard_map/dot_general | solution.py:25
  85.5 3.0 %copy-done.2 = bf16[4096,896]{1,0:T(8,128)(2,1)} copy-done((bf16[4096,896]{1,0:T(8,128)(2,1)}, bf16[4096,896]{1,0:T(8,128)(2,1)S(1)}, u32[]{:S(2)}) %copy-start.2) | copy-done | bytes 7340056
  88.5 2.3 %fusion = bf16[2,4,256,896]{3,2,1,0:T(8,128)(2,1)} fusion(bf16[2,4,2,256,896]{4,3,2,1,0:T(8,128)(2,1)S(1)} %bitcast.49, s32[]{:T(128)S(6)} %select_n.90, pred[]{:T(512)S(6)} %and.53), kind=kLoop, calls=%fused_computation.5 | loop fusion | flops 1835008 | bytes 7340037 | tf_op jit(solution)/shard_map/jit(_take)/select_n | solution.py:32
  90.8 0.8 collective-permute-start.1
  91.6 6.4 %collective-permute-done.1 = bf16[2,4,256,896]{3,2,1,0:T(8,128)(2,1)} collective-permute-done((bf16[2,4,256,896]{3,2,1,0:T(8,128)(2,1)}, bf16[2,4,256,896]{3,2,1,0:T(8,128)(2,1)}, u32[]{:S(2)}, u32[]{:S(2)}) %collective-permute-start.1) | collective-permute-done | bytes 3670048 | tf_op jit(solution)/shard_map/ppermute | solution.py:19
  98.0 4.3 %convert_add_fusion = f32[2,4,256,896]{3,2,1,0:T(8,128)S(1)} fusion(bf16[2,4,256,896]{3,2,1,0:T(8,128)(2,1)} %collective-permute-done.1, bf16[2,4,2,256,896]{4,3,2,1,0:T(8,128)(2,1)} %bitcast.50, s32[]{:T(128)S(6)} %select_n.88, pred[]{:T(512)S(6)} %and.52), kind=kLoop, calls=%fused_computation.1 | loop fusion | flops 7340032 | bytes 14680069 | tf_op jit(solution)/shard_map/add | solution.py:33
  102.3 3.0 %copy-done = f32[2,4,256,896]{3,2,1,0:T(8,128)} copy-done((f32[2,4,256,896]{3,2,1,0:T(8,128)}, f32[2,4,256,896]{3,2,1,0:T(8,128)S(1)}, u32[]{:S(2)}) %copy-start) | copy-done | bytes 7340056
  105.4 1.6 select_bitcast_fusion.2
  107.0 2.4 %collective-permute-start.4 = (bf16[2,256,896]{2,1,0:T(8,128)(2,1)}, bf16[2,256,896]{2,1,0:T(8,128)(2,1)}, u32[]{:S(2)}, u32[]{:S(2)}) collective-permute-start(bf16[2,256,896]{2,1,0:T(8,128)(2,1)} %get-tuple-element.70), channel_id=1, source_target_pairs={{0,96},{32,0},{64,32},{96,64},{1,97},{33,1},{65,33},{97,65},{2,98}... | collective-permute-start | bytes 2752520 | tf_op jit(solution)/shard_map/ppermute | solution.py:19
  109.4 0.6 collective-permute-start.3
  110.0 0.6 collective-permute-start.2
  110.6 6.3 %fusion.11 = (bf16[512,896]{1,0:T(8,128)(2,1)}, bf16[512,896]{1,0:T(8,128)(2,1)}) fusion(bf16[512,896]{1,0:T(8,128)(2,1)S(1)} %copy-done.9, bf16[512,896]{1,0:T(8,128)(2,1)S(1)} %copy-done.7, bf16[512,4096]{1,0:T(8,128)(2,1)S(1)} %copy-done.5, bf16[896,4096]{1,0:T(8,128)(2,1)S(1)} %bitcast.48), kind=kOutput, calls=%fused_computation.23 | convolution fusion | flops 3764977664 | bytes 15204352 | tf_op jit(solution)/shard_map/dot_general | solution.py:68
  116.9 18.0 %reduce-scatter.2.cloned.1.call-done = bf16[64,4096]{1,0:T(8,128)(2,1)} async-done(((bf16[512,4096]{1,0:T(8,128)(2,1)}), bf16[64,4096]{1,0:T(8,128)(2,1)}) %reduce-scatter.2.cloned.1.call-update) | async-done | bytes 524304 | tf_op jit(solution)/shard_map/reduce_scatter | solution.py:57
  134.8 1.0 constant_dynamic-slice_fusion
  135.8 2.8 %collective-permute-start = (bf16[32,4096]{1,0:T(8,128)(2,1)S(1)}, bf16[32,4096]{1,0:T(8,128)(2,1)S(1)}, u32[]{:S(2)}, u32[]{:S(2)}) collective-permute-start(bf16[32,4096]{1,0:T(8,128)(2,1)S(1)} %constant_dynamic-slice_fusion), channel_id=1, source_target_pairs={{0,1},{1,0},{2,3},{3,2},{4,5},{5,4},{6,7},{7,6},{8,9},{9,8},{10,11... | collective-permute-start | bytes 786440 | tf_op jit(solution)/shard_map/ppermute | solution.py:19
  138.6 14.5 %collective-permute-done.2 = bf16[2,256,896]{2,1,0:T(8,128)(2,1)} collective-permute-done((bf16[2,256,896]{2,1,0:T(8,128)(2,1)}, bf16[2,256,896]{2,1,0:T(8,128)(2,1)}, u32[]{:S(2)}, u32[]{:S(2)}) %collective-permute-start.2) | collective-permute-done | bytes 917536 | tf_op jit(solution)/shard_map/ppermute | solution.py:19
  153.2 2.8 %fusion.13 = f32[2,256,896]{2,1,0:T(8,128)S(1)} fusion(s32[]{:T(128)S(6)} %select_n.60, bf16[2,256,896]{2,1,0:T(8,128)(2,1)} %collective-permute-done.4, bf16[2,256,896]{2,1,0:T(8,128)(2,1)} %collective-permute-done.3, bf16[2,256,896]{2,1,0:T(8,128)(2,1)} %collective-permute-done.2, pred[]{:T(512)S(6)} %and.50, f32[2,4,256,896]{3,2,1,0:T(8,128)} %copy-done), kind=kLoop, calls=%fused_computation.26 | loop fusion | flops 3211264 | bytes 6422533 | tf_op jit(solution)/shard_map/add | solution.py:40
  155.9 0.1 fusion.17
  156.0 1.3 collective-permute-start.5
  157.3 0.8 add_convert_fusion
  158.1 9.6 %collective-permute-done.5 = bf16[256,896]{1,0:T(8,128)(2,1)S(1)} collective-permute-done((bf16[256,896]{1,0:T(8,128)(2,1)S(1)}, bf16[256,896]{1,0:T(8,128)(2,1)S(1)}, u32[]{:S(2)}, u32[]{:S(2)}) %collective-permute-start.5) | collective-permute-done | bytes 458784 | tf_op jit(solution)/shard_map/ppermute | solution.py:19
  167.7 0.1 fusion.15
  167.8 1.0 copy.16
  (27 shorter events, 0.1 us)
Async XLA Ops:
  7.2 14.3 %copy-start.3 = (s32[28,4096]{1,0:T(8,128)S(1)}, s32[28,4096]{1,0:T(8,128)}, u32[]{:S(2)}) copy-start(s32[28,4096]{1,0:T(8,128)} %param.13) | copy-start | bytes 1376260
  7.2 71.1 %all-gather.2.cloned.1.call-start = ((), (), s32[]{:S(2)}) async-start(), calls=%async_computation.3 | async-start | bytes 4718592 | tf_op jit(solution)/shard_map/all_gather | solution.py:67
  21.4 113.4 %reduce-scatter.2.cloned.1.call-start = ((), (), s32[]{:S(2)}) async-start(), calls=%async_computation.2 | async-start | bytes 4718592 | tf_op jit(solution)/shard_map/reduce_scatter | solution.py:57
  25.3 2.9 %copy-start.1 = (bf16[896,4096]{1,0:T(8,128)(2,1)}, bf16[896,4096]{1,0:T(8,128)(2,1)S(1)}, u32[]{:S(2)}) copy-start(bf16[896,4096]{1,0:T(8,128)(2,1)S(1)} %bitcast_multiply_fusion) | copy-start | bytes 22020100
  36.0 42.2 %copy-start.6 = (bf16[512,896]{1,0:T(8,128)(2,1)S(1)}, bf16[512,896]{1,0:T(8,128)(2,1)}, u32[]{:S(2)}) copy-start(bf16[512,896]{1,0:T(8,128)(2,1)} %param.10) | copy-start | bytes 2752516
  36.0 42.2 %copy-start.8 = (bf16[512,896]{1,0:T(8,128)(2,1)S(1)}, bf16[512,896]{1,0:T(8,128)(2,1)}, u32[]{:S(2)}) copy-start(bf16[512,896]{1,0:T(8,128)(2,1)} %param.9) | copy-start | bytes 2752516
  85.5 3.0 %copy-start.2 = (bf16[4096,896]{1,0:T(8,128)(2,1)}, bf16[4096,896]{1,0:T(8,128)(2,1)S(1)}, u32[]{:S(2)}) copy-start(bf16[4096,896]{1,0:T(8,128)(2,1)S(1)} %convolution_convert_fusion) | copy-start | bytes 22020100
  88.5 22.1 %slice-start = ((s8[7340032]{0:T(1024)(128)(4,1)}), s8[3145728]{0:T(1024)(128)(4,1)S(1)}, s32[]{:S(2)}) async-start(s8[7340032]{0:T(1024)(128)(4,1)} %bitcast.47), calls=%async_computation.4 | async-start | bytes 6291456
  90.8 7.2 %collective-permute-start.1 = (bf16[2,4,256,896]{3,2,1,0:T(8,128)(2,1)}, bf16[2,4,256,896]{3,2,1,0:T(8,128)(2,1)}, u32[]{:S(2)}, u32[]{:S(2)}) collective-permute-start(bf16[2,4,256,896]{3,2,1,0:T(8,128)(2,1)} %fusion), channel_id=1, source_target_pairs={{0,16},{16,0},{1,17},{17,1},{2,18},{18,2},{3,19},{19,3},{4,20},{20... | collective-permute-start | bytes 11010056 | tf_op jit(solution)/shard_map/ppermute | solution.py:19
  91.6 18.9 %slice-start.1 = ((s8[7340032]{0:T(1024)(128)(4,1)}), s8[4194304]{0:T(1024)(128)(4,1)S(1)}, s32[]{:S(2)}) async-start(s8[7340032]{0:T(1024)(128)(4,1)} %bitcast.47), calls=%async_computation.5 | async-start | bytes 8388608
  98.0 12.5 %copy-start.9 = (bf16[512,896]{1,0:T(8,128)(2,1)S(1)}, bf16[512,896]{1,0:T(8,128)(2,1)}, u32[]{:S(2)}) copy-start(bf16[512,896]{1,0:T(8,128)(2,1)} %param.9) | copy-start | bytes 2752516
  102.3 3.0 %copy-start = (f32[2,4,256,896]{3,2,1,0:T(8,128)}, f32[2,4,256,896]{3,2,1,0:T(8,128)S(1)}, u32[]{:S(2)}) copy-start(f32[2,4,256,896]{3,2,1,0:T(8,128)S(1)} %convert_add_fusion) | copy-start | bytes 22020100
  105.4 5.2 %copy-start.5 = (bf16[512,4096]{1,0:T(8,128)(2,1)S(1)}, bf16[512,4096]{1,0:T(8,128)(2,1)}, u32[]{:S(2)}) copy-start(bf16[512,4096]{1,0:T(8,128)(2,1)} %all-gather.2.cloned.1.call-done) | copy-start | bytes 12582916
  105.4 5.2 %copy-start.7 = (bf16[512,896]{1,0:T(8,128)(2,1)S(1)}, bf16[512,896]{1,0:T(8,128)(2,1)}, u32[]{:S(2)}) copy-start(bf16[512,896]{1,0:T(8,128)(2,1)} %param.10) | copy-start | bytes 2752516
  107.0 31.6 %collective-permute-start.4 = (bf16[2,256,896]{2,1,0:T(8,128)(2,1)}, bf16[2,256,896]{2,1,0:T(8,128)(2,1)}, u32[]{:S(2)}, u32[]{:S(2)}) collective-permute-start(bf16[2,256,896]{2,1,0:T(8,128)(2,1)} %get-tuple-element.70), channel_id=1, source_target_pairs={{0,96},{32,0},{64,32},{96,64},{1,97},{33,1},{65,33},{97,65},{2,98}... | collective-permute-start | bytes 2752520 | tf_op jit(solution)/shard_map/ppermute | solution.py:19
  109.4 29.2 %collective-permute-start.3 = (bf16[2,256,896]{2,1,0:T(8,128)(2,1)}, bf16[2,256,896]{2,1,0:T(8,128)(2,1)}, u32[]{:S(2)}, u32[]{:S(2)}) collective-permute-start(bf16[2,256,896]{2,1,0:T(8,128)(2,1)} %get-tuple-element.71), channel_id=1, source_target_pairs={{0,64},{32,96},{64,0},{96,32},{1,65},{33,97},{65,1},{97,33},{2,66}... | collective-permute-start | bytes 2752520 | tf_op jit(solution)/shard_map/ppermute | solution.py:19
  110.0 43.2 %collective-permute-start.2 = (bf16[2,256,896]{2,1,0:T(8,128)(2,1)}, bf16[2,256,896]{2,1,0:T(8,128)(2,1)}, u32[]{:S(2)}, u32[]{:S(2)}) collective-permute-start(bf16[2,256,896]{2,1,0:T(8,128)(2,1)} %get-tuple-element.69), channel_id=1, source_target_pairs={{0,32},{32,64},{64,96},{96,0},{1,33},{33,65},{65,97},{97,1},{2,34}... | collective-permute-start | bytes 2752520 | tf_op jit(solution)/shard_map/ppermute | solution.py:19
  135.8 21.5 %copy-start.4 = (bf16[64,4096]{1,0:T(8,128)(2,1)S(1)}, bf16[64,4096]{1,0:T(8,128)(2,1)}, u32[]{:S(2)}) copy-start(bf16[64,4096]{1,0:T(8,128)(2,1)} %reduce-scatter.2.cloned.1.call-done) | copy-start | bytes 1572868
  135.8 21.5 %collective-permute-start = (bf16[32,4096]{1,0:T(8,128)(2,1)S(1)}, bf16[32,4096]{1,0:T(8,128)(2,1)S(1)}, u32[]{:S(2)}, u32[]{:S(2)}) collective-permute-start(bf16[32,4096]{1,0:T(8,128)(2,1)S(1)} %constant_dynamic-slice_fusion), channel_id=1, source_target_pairs={{0,1},{1,0},{2,3},{3,2},{4,5},{5,4},{6,7},{7,6},{8,9},{9,8},{10,11... | collective-permute-start | bytes 786440 | tf_op jit(solution)/shard_map/ppermute | solution.py:19
  156.0 11.7 %collective-permute-start.5 = (bf16[256,896]{1,0:T(8,128)(2,1)S(1)}, bf16[256,896]{1,0:T(8,128)(2,1)S(1)}, u32[]{:S(2)}, u32[]{:S(2)}) collective-permute-start(bf16[256,896]{1,0:T(8,128)(2,1)S(1)} %fusion.17), channel_id=1, source_target_pairs={{0,128},{128,0},{1,129},{129,1},{2,130},{130,2},{3,131},{131,3},{4... | collective-permute-start | bytes 1376264 | tf_op jit(solution)/shard_map/ppermute | solution.py:19
Sparse Core Ops, SparseCore 0:
  21.6 56.6 all-gather.1
  80.8 54.0 reduce-scatter.1
